TPU v7x, 32 devices: a whole 2x2x4 slice. The times are simulated.
32 devices in a mesh: grp: 8 (over z, y), band: 4 (over x, core).
Axes of the slice: x: 2, y: 2, z: 4, core: 2. Of those that a mesh axis runs over, the one named last changes fastest.
Arguments:
- x_blocks: bfloat16 [4, 4, 64, 8192], P('band', None, None, 'grp'), may hold values from -6 to 6
- pair_ids: int32 [8, 4, 4], P('grp', 'band'), may hold values from 0 to 15, as said below
- live_count: int32 [8, 4], P('grp', 'band'), may hold values from 2 to 4, as said below
- green_occ: bfloat16 [512, 512], replicated, may hold values from -0.0234375 to 0.0234375
- green_virt: bfloat16 [512, 512], replicated, may hold values from -0.0234375 to 0.0234375
Outputs:
- chi: float32 [128, 128], P(('grp', 'band'))
Inputs may be any that keep to these rules, and one draw needn't show every extreme that they name: On each device the 4 codes pair_ids[g, b, :] are distinct; code e names mu block e // 2 and nu block 2 * b + e % 2. `live_count`: in every draw some device has all 4 slots live.
All inputs are finite; a program needn't handle non-finite values.
Results may differ from a plain program's by a relative error of at most 0.0041.
Values may be sent and summed in bfloat16 or wider, within the bound.
No kernel may reach another device: no remote copies, remote signals or barrier semaphores. Data moves between devices by JAX's collectives and lax.ppermute only.
A program may use at most 128 MiB of HBM per device.

v0:
```python
import jax
import jax.numpy as jnp
from jax import lax
from jax.sharding import PartitionSpec as P


def on_device(x_blocks, pair_ids, live_count, green_occ, green_virt):
    local_blocks = x_blocks[0]
    pair_list = pair_ids[0, 0]
    live_slots = live_count[0, 0]
    slot_count = local_blocks.shape[0]
    block_size = local_blocks.shape[1]
    ri_cols = local_blocks.shape[2]
    ri_local = ri_cols // block_size
    orbitals = green_occ.shape[0]
    band_orbs = 2 * block_size
    band_count = lax.axis_size("band")
    group_count = lax.axis_size("grp")
    ri_total = ri_local * group_count
    mu_blocks = pair_list // 2
    half_codes = pair_list % 2
    slot_index = jnp.arange(slot_count, dtype=jnp.int32)
    row_index = (
        mu_blocks[:, None] * block_size + jnp.arange(block_size, dtype=jnp.int32)[None, :]
    ).reshape(-1)
    occ_rows = jnp.take(green_occ, row_index, axis=0).reshape(slot_count, block_size, orbitals)
    virt_rows = jnp.take(green_virt, row_index, axis=0).reshape(slot_count, block_size, orbitals)
    live_mask = slot_index < live_slots
    occ_halves = []
    virt_halves = []
    for half in range(2):
        weight = jnp.logical_and(live_mask, half_codes == half).astype(jnp.bfloat16)[:, None, None]
        occ_sel = occ_rows * weight
        virt_sel = virt_rows * weight
        occ_part = lax.dot_general(
            local_blocks, occ_sel, (((0, 1), (0, 1)), ((), ())), preferred_element_type=jnp.float32
        )
        virt_part = lax.dot_general(
            virt_sel, local_blocks, (((0, 1), (0, 1)), ((), ())), preferred_element_type=jnp.float32
        )
        occ_halves.append(occ_part.astype(jnp.bfloat16).reshape(ri_local, 1, block_size, orbitals))
        virt_halves.append(
            virt_part.astype(jnp.bfloat16).reshape(orbitals, ri_local, 1, block_size)
        )
    occ_three = jnp.concatenate(occ_halves, axis=1).reshape(ri_local, band_orbs, orbitals)
    virt_three = jnp.concatenate(virt_halves, axis=2).reshape(orbitals, ri_local, band_orbs)
    moved = lax.all_to_all(
        occ_three.reshape(ri_local, 1, band_orbs, band_count, band_orbs),
        "band",
        split_axis=3,
        concat_axis=1,
        tiled=True,
    )
    moved = moved.reshape(ri_local, orbitals, band_orbs)
    pair_cols = orbitals // group_count
    occ_pairs = lax.all_to_all(
        moved.reshape(ri_local, group_count, pair_cols, band_orbs),
        "grp",
        split_axis=1,
        concat_axis=0,
        tiled=True,
    )
    occ_pairs = occ_pairs.reshape(ri_total, pair_cols, band_orbs)
    virt_pairs = lax.all_to_all(
        virt_three.reshape(group_count, pair_cols, ri_local, band_orbs),
        "grp",
        split_axis=0,
        concat_axis=2,
        tiled=True,
    )
    virt_pairs = virt_pairs.reshape(pair_cols, ri_total, band_orbs)
    partial_value = lax.dot_general(
        occ_pairs, virt_pairs, (((1, 2), (0, 2)), ((), ())), preferred_element_type=jnp.float32
    )
    group_sum = lax.psum_scatter(partial_value, "grp", scatter_dimension=0, tiled=True)
    response = lax.psum_scatter(group_sum, "band", scatter_dimension=0, tiled=True)
    return response


def solution(mesh):
    placed = (P("band", None, None, "grp"), P("grp", "band", None), P("grp", "band"), P(), P())
    return jax.shard_map(
        on_device, mesh=mesh, in_specs=placed, out_specs=P(("grp", "band"), None), check_vma=False
    )
```

profile of v0, /device:TPU:0, one launch (start us, length us, event | category | flops | bytes accessed | tf_op | source)
XLA Modules:
  0.0 237.8 jit_solution(10687282440000746870)
XLA Ops:
  8.8 2.3 gather_fusion
  11.1 1.2 gather_fusion.1
  13.8 1.4 fusion
  15.2 1.5 copy.15
  17.2 2.1 reshape_reshape.9
  19.3 3.4 %copy.18 = bf16[16,1,128,4,128]{4,2,0,1,3:T(8,128)(2,1)} copy(bf16[16,1,128,4,128]{4,3,2,0,1:T(4,128)(2,1)} %reshape_reshape.9) | data formatting | bytes 4194304 | tf_op jit(solution)/shard_map/reshape;reshape | solution.py:48
  22.7 4.5 %all-to-all-start = ((bf16[16,1,128,4,128]{4,2,0,1,3:T(8,128)(2,1)}), bf16[16,1,128,4,128]{4,2,0,1,3:T(8,128)(2,1)}, u32[]{:S(2)}, u32[]{:S(2)}) async-start(bf16[16,1,128,4,128]{4,2,0,1,3:T(8,128)(2,1)} %copy.18), calls=%async_computation | async-start | bytes 4194304 | tf_op jit(solution)/shard_map/all_to_all | solution.py:47
  27.6 1.3 copy.22
  29.4 1.3 copy.23
  30.7 1.7 pad_maximum_fusion.1
  32.5 7.7 %copy.27 = bf16[512,16,2,64]{3,2,1,0:T(2,128)(2,1)} copy(bf16[512,16,2,64]{0,3,1,2:T(8,128)(2,1)S(1)} %pad_maximum_fusion.1) | data formatting | bytes 4194304 | tf_op jit(solution)/shard_map/reshape;reshape | solution.py:65
  40.1 7.8 %reshape.143 = bf16[8,64,16,128]{3,2,1,0:T(8,128)(2,1)} reshape(bf16[512,16,2,64]{3,2,1,0:T(2,128)(2,1)} %copy.27) | data formatting | bytes 4194304 | tf_op jit(solution)/shard_map/reshape;reshape | solution.py:65
  47.9 5.6 %all-to-all-done = bf16[16,1,128,4,128]{4,2,0,1,3:T(8,128)(2,1)} async-done(((bf16[16,1,128,4,128]{4,2,0,1,3:T(8,128)(2,1)}), bf16[16,1,128,4,128]{4,2,0,1,3:T(8,128)(2,1)}, u32[]{:S(2)}, u32[]{:S(2)}) %all-to-all-start) | async-done | bytes 2097184 | tf_op jit(solution)/shard_map/all_to_all | solution.py:47
  53.6 6.7 %all-to-all-start.2 = ((bf16[8,64,16,128]{3,2,1,0:T(8,128)(2,1)}), bf16[8,64,16,128]{3,2,1,0:T(8,128)(2,1)S(1)}, u32[]{:S(2)}, u32[]{:S(2)}) async-start(bf16[8,64,16,128]{3,2,1,0:T(8,128)(2,1)} %reshape.143), calls=%async_computation.2 | async-start | bytes 4194304 | tf_op jit(solution)/shard_map/all_to_all | solution.py:64
  60.2 1.7 copy.19
  62.0 1.5 copy.20
  63.5 44.8 %all-to-all-done.2 = bf16[8,64,16,128]{3,2,1,0:T(8,128)(2,1)S(1)} async-done(((bf16[8,64,16,128]{3,2,1,0:T(8,128)(2,1)}), bf16[8,64,16,128]{3,2,1,0:T(8,128)(2,1)S(1)}, u32[]{:S(2)}, u32[]{:S(2)}) %all-to-all-start.2) | async-done | bytes 2097184 | tf_op jit(solution)/shard_map/all_to_all | solution.py:64
  108.3 4.3 %all-to-all-start.1 = ((bf16[16,8,64,128]{3,2,0,1:T(8,128)(2,1)}), bf16[16,8,64,128]{3,2,0,1:T(8,128)(2,1)}, u32[]{:S(2)}, u32[]{:S(2)}) async-start(bf16[16,8,64,128]{3,2,0,1:T(8,128)(2,1)} %copy.20), calls=%async_computation.1 | async-start | bytes 4194304 | tf_op jit(solution)/shard_map/all_to_all | solution.py:56
  112.7 1.9 copy.26
  114.6 45.8 %all-to-all-done.1 = bf16[16,8,64,128]{3,2,0,1:T(8,128)(2,1)} async-done(((bf16[16,8,64,128]{3,2,0,1:T(8,128)(2,1)}), bf16[16,8,64,128]{3,2,0,1:T(8,128)(2,1)}, u32[]{:S(2)}, u32[]{:S(2)}) %all-to-all-start.1) | async-done | bytes 2097184 | tf_op jit(solution)/shard_map/all_to_all | solution.py:56
  160.4 3.1 %copy.21 = bf16[8,16,1,64,128]{4,1,0,3,2:T(8,128)(2,1)S(1)} copy(bf16[8,16,1,64,128]{4,3,1,0,2:T(8,128)(2,1)} %bitcast.15) | data formatting | bytes 4194304 | tf_op jit(solution)/shard_map/all_to_all | solution.py:56
  163.6 1.3 convolution_bitcast_fusion
  166.2 58.3 %reduce-scatter.2.cloned.1.call-done = f32[16,128]{1,0:T(8,128)} async-done(((f32[128,128]{1,0:T(8,128)}), f32[16,128]{1,0:T(8,128)}) %reduce-scatter.2.cloned.1.call-update) | async-done | bytes 8208 | tf_op jit(solution)/shard_map/reduce_scatter | solution.py:75
  224.5 5.9 %all-reduce = f32[16,128]{1,0:T(8,128)S(1)} all-reduce(f32[16,128]{1,0:T(8,128)} %reduce-scatter.2.cloned.1.call-done), channel_id=3, replica_groups=mesh['grp'=8,'band'=4] {'band'}, use_global_device_ids=true, to_apply=%region_1.3.clone | all-reduce | flops 2048 | bytes 16384
  (31 shorter events, 5.6 us)
Async XLA Ops:
  6.5 6.3 %copy-start = (bf16[1,4,64,1024]{3,2,1,0:T(8,128)(2,1)S(1)}, bf16[1,4,64,1024]{3,2,1,0:T(8,128)(2,1)}, u32[]{:S(2)}) copy-start(bf16[1,4,64,1024]{3,2,1,0:T(8,128)(2,1)} %param.7) | copy-start | bytes 1572868
  6.5 4.6 %copy-start.2 = (bf16[512,512]{1,0:T(8,128)(2,1)S(1)}, bf16[512,512]{1,0:T(8,128)(2,1)}, u32[]{:S(2)}) copy-start(bf16[512,512]{1,0:T(8,128)(2,1)} %param.11) | copy-start | bytes 1572868
  22.7 30.9 %all-to-all-start = ((bf16[16,1,128,4,128]{4,2,0,1,3:T(8,128)(2,1)}), bf16[16,1,128,4,128]{4,2,0,1,3:T(8,128)(2,1)}, u32[]{:S(2)}, u32[]{:S(2)}) async-start(bf16[16,1,128,4,128]{4,2,0,1,3:T(8,128)(2,1)} %copy.18), calls=%async_computation | async-start | bytes 4194304 | tf_op jit(solution)/shard_map/all_to_all | solution.py:47
  53.6 54.7 %all-to-all-start.2 = ((bf16[8,64,16,128]{3,2,1,0:T(8,128)(2,1)}), bf16[8,64,16,128]{3,2,1,0:T(8,128)(2,1)S(1)}, u32[]{:S(2)}, u32[]{:S(2)}) async-start(bf16[8,64,16,128]{3,2,1,0:T(8,128)(2,1)} %reshape.143), calls=%async_computation.2 | async-start | bytes 4194304 | tf_op jit(solution)/shard_map/all_to_all | solution.py:64
  108.3 52.2 %all-to-all-start.1 = ((bf16[16,8,64,128]{3,2,0,1:T(8,128)(2,1)}), bf16[16,8,64,128]{3,2,0,1:T(8,128)(2,1)}, u32[]{:S(2)}, u32[]{:S(2)}) async-start(bf16[16,8,64,128]{3,2,0,1:T(8,128)(2,1)} %copy.20), calls=%async_computation.1 | async-start | bytes 4194304 | tf_op jit(solution)/shard_map/all_to_all | solution.py:56
  112.6 111.9 %reduce-scatter.2.cloned.1.call-start = ((), (), s32[]{:S(2)}) async-start(), calls=%async_computation.4 | async-start | bytes 73728 | tf_op jit(solution)/shard_map/reduce_scatter | solution.py:75
  160.4 3.1 %copy-start.1 = (bf16[1,64,8,16,128]{4,3,2,1,0:T(8,128)(2,1)S(1)}, bf16[1,64,8,16,128]{4,3,2,1,0:T(8,128)(2,1)}, u32[]{:S(2)}) copy-start(bf16[1,64,8,16,128]{4,3,2,1,0:T(8,128)(2,1)} %copy.26) | copy-start | bytes 6291460
  163.6 1.4 copy-start.3
Sparse Core Ops, SparseCore 0:
  165.0 59.4 reduce-scatter.1
where the time goes:
time: 239 us; the launch traced here: 238 us
  waiting for transfers between devices  155 us (65%)
  local copies, waits for them, and re-layouts  39.2 us (16%)
  starting transfers between devices  15.5 us (6%)
  between operations  15 us (6%)
  blocking collectives  5.87 us (2%)
  matrix products  4.12 us (2%)
  other arithmetic  3.53 us (1%)
    reduce_scatter x1, waiting for transfers between devices, on_device(): lax.psum_scatter(partial_value, 'grp', scatter_dimension=0, tiled=True)  58.3 us
    all_to_all x1, waiting for transfers between devices, on_device(): lax.all_to_all(moved.reshape(ri_local, group_count, pair_cols, band_orbs)...  45.8 us
    all_to_all x1, waiting for transfers between devices, on_device(): lax.all_to_all(virt_three.reshape(group_count, pair_cols, ri_local, band_...  44.8 us
    another operation x2, local copies, waits for them, and re-layouts, on_device(): virt_three.reshape(group_count, pair_cols, ri_local, band_orbs)  15.4 us
    all_to_all x1, starting transfers between devices, on_device(): lax.all_to_all(virt_three.reshape(group_count, pair_cols, ri_local, band_...  6.66 us
    unnamed x1, blocking collectives  5.87 us
    all_to_all x1, waiting for transfers between devices, on_device(): lax.all_to_all(occ_three.reshape(ri_local, 1, band_orbs, band_count, band...  5.64 us
    another operation x2, local copies, waits for them, and re-layouts, on_device(): occ_three.reshape(ri_local, 1, band_orbs, band_count, band_orbs)  5.53 us
  transfers between devices with their start and end apart: 4, of which 4 were waited for; matrix products, arithmetic and copies ran while one was open for 11% of the time, Pallas kernels for 0%

commit v1 on v0

--- a/solution.py
+++ b/solution.py
@@ -53,13 +53,20 @@
     )
     moved = moved.reshape(ri_local, orbitals, band_orbs)
     pair_cols = orbitals // group_count
-    occ_pairs = lax.all_to_all(
-        moved.reshape(ri_local, group_count, pair_cols, band_orbs),
-        "grp",
-        split_axis=1,
-        concat_axis=0,
-        tiled=True,
-    )
+    x = moved.reshape(ri_local, group_count, pair_cols, band_orbs)
+    ways, here = (lax.axis_size("grp"), lax.axis_index("grp"))
+    width = x.shape[1] // ways
+    lengths = list(x.shape)
+    lengths[1] = width
+    height = lengths[0]
+    lengths[0] = height * ways
+    full = jnp.zeros(lengths, x.dtype)
+    for mask in range(ways):
+        part = lax.dynamic_slice_in_dim(x, (here ^ mask) * width, width, axis=1)
+        if mask:
+            part = lax.ppermute(part, "grp", [(d, d ^ mask) for d in range(ways)])
+        full = lax.dynamic_update_slice_in_dim(full, part, (here ^ mask) * height, axis=0)
+    occ_pairs = full
     occ_pairs = occ_pairs.reshape(ri_total, pair_cols, band_orbs)
     virt_pairs = lax.all_to_all(
         virt_three.reshape(group_count, pair_cols, ri_local, band_orbs),

time: 239 us -> 231 us (0.967)
  waiting for transfers between devices: 155 us -> 128 us
  starting transfers between devices: 15.5 us -> 28.2 us
  local copies, waits for them, and re-layouts: 39.2 us -> 44.5 us
    ppermute x0 -> x7, waiting for transfers between devices: none -> 56.5 us  [on_device(): part = lax.ppermute(part, 'grp', [(d, d ^ mask) for d in range(ways)])]
    all_to_all x1 -> x0, waiting for transfers between devices: 45.8 us -> none  [on_device(): lax.all_to_all(moved.reshape(ri_local, group_count, pair_cols, band_orbs)...]
    all_to_all x1, waiting for transfers between devices: 44.8 us -> 0.01 us  [on_device(): lax.all_to_all(virt_three.reshape(group_count, pair_cols, ri_local, band_...]
    ppermute x0 -> x7, starting transfers between devices: none -> 17 us  [on_device(): part = lax.ppermute(part, 'grp', [(d, d ^ mask) for d in range(ways)])]
    dynamic_update_slice x0 -> x8, local copies, waits for them, and re-layouts: none -> 8.22 us  [on_device(): lax.dynamic_update_slice_in_dim(full, part, (here ^ mask) * height, axis=0)]
    reduce_scatter x1, waiting for transfers between devices: 58.3 us -> 65.7 us  [on_device(): lax.psum_scatter(partial_value, 'grp', scatter_dimension=0, tiled=True)]
    all_to_all x1 -> x0, starting transfers between devices: 4.35 us -> none  [on_device(): lax.all_to_all(moved.reshape(ri_local, group_count, pair_cols, band_orbs)...]
    all_to_all x1 -> x0, local copies, waits for them, and re-layouts: 3.09 us -> none  [on_device(): lax.all_to_all(moved.reshape(ri_local, group_count, pair_cols, band_orbs)...]
  transfers between devices with their start and end apart: 4 -> 10, of which waited for: 4 -> 7; matrix products, arithmetic and copies ran while one was open for 11% -> 15% of each run, Pallas kernels for 0% -> 0%
where the time goes in v1:
time: 231 us
  waiting for transfers between devices  128 us (55%)
  local copies, waits for them, and re-layouts  44.5 us (19%)
  starting transfers between devices  28.2 us (12%)
  between operations  15 us (6%)
  blocking collectives  5.87 us (3%)
  matrix products  5.75 us (2%)
  other arithmetic  3.53 us (2%)
    reduce_scatter x1, waiting for transfers between devices, on_device(): lax.psum_scatter(partial_value, 'grp', scatter_dimension=0, tiled=True)  65.7 us
    ppermute x7, waiting for transfers between devices, on_device(): part = lax.ppermute(part, 'grp', [(d, d ^ mask) for d in range(ways)])  56.5 us
    ppermute x7, starting transfers between devices, on_device(): part = lax.ppermute(part, 'grp', [(d, d ^ mask) for d in range(ways)])  17 us
    another operation x2, local copies, waits for them, and re-layouts, on_device(): virt_three.reshape(group_count, pair_cols, ri_local, band_orbs)  15.5 us
    dynamic_update_slice x8, local copies, waits for them, and re-layouts, on_device(): lax.dynamic_update_slice_in_dim(full, part, (here ^ mask) * height, axis=0)  8.22 us
    all_to_all x1, starting transfers between devices, on_device(): lax.all_to_all(virt_three.reshape(group_count, pair_cols, ri_local, band_...  6.7 us
    unnamed x1, blocking collectives  5.87 us
    all_to_all x1, waiting for transfers between devices, on_device(): lax.all_to_all(occ_three.reshape(ri_local, 1, band_orbs, band_count, band...  5.54 us
  transfers between devices with their start and end apart: 10, of which 7 were waited for; matrix products, arithmetic and copies ran while one was open for 15% of the time, Pallas kernels for 0%

profile of v1, /device:TPU:0, one launch (start us, length us, event | category | flops | bytes accessed | tf_op | source)
XLA Modules:
  0.0 230.5 jit_solution(2056220244586961029)
XLA Ops:
  8.8 2.3 %gather_fusion = bf16[256,512]{1,0:T(8,128)(2,1)S(1)} fusion(bf16[512,512]{1,0:T(8,128)(2,1)} %param.10, s32[1024]{0:T(1024)S(1)} %pad_clamp_fusion), kind=kCustom, calls=%fused_computation.clone | custom fusion | bytes 525312 | tf_op jit(solution)/shard_map/jit(_take)/gather | solution.py:26
  15.3 1.5 copy.44
  17.2 2.1 reshape_reshape.9
  19.3 3.5 %copy.47 = bf16[16,1,128,4,128]{4,2,0,1,3:T(8,128)(2,1)} copy(bf16[16,1,128,4,128]{4,3,2,0,1:T(4,128)(2,1)} %reshape_reshape.9) | data formatting | bytes 4194304 | tf_op jit(solution)/shard_map/reshape;reshape | solution.py:48
  22.7 4.5 %all-to-all-start = ((bf16[16,1,128,4,128]{4,2,0,1,3:T(8,128)(2,1)}), bf16[16,1,128,4,128]{4,2,0,1,3:T(8,128)(2,1)}, u32[]{:S(2)}, u32[]{:S(2)}) async-start(bf16[16,1,128,4,128]{4,2,0,1,3:T(8,128)(2,1)} %copy.47), calls=%async_computation | async-start | bytes 4194304 | tf_op jit(solution)/shard_map/all_to_all | solution.py:47
  30.8 1.7 pad_maximum_fusion.1
  32.5 7.7 %copy.62 = bf16[512,16,2,64]{3,2,1,0:T(2,128)(2,1)} copy(bf16[512,16,2,64]{0,3,1,2:T(8,128)(2,1)S(1)} %pad_maximum_fusion.1) | data formatting | bytes 4194304 | tf_op jit(solution)/shard_map/reshape;reshape | solution.py:72
  40.2 7.8 %reshape.182 = bf16[8,64,16,128]{3,2,1,0:T(8,128)(2,1)} reshape(bf16[512,16,2,64]{3,2,1,0:T(2,128)(2,1)} %copy.62) | data formatting | bytes 4194304 | tf_op jit(solution)/shard_map/reshape;reshape | solution.py:72
  48.0 5.5 %all-to-all-done = bf16[16,1,128,4,128]{4,2,0,1,3:T(8,128)(2,1)} async-done(((bf16[16,1,128,4,128]{4,2,0,1,3:T(8,128)(2,1)}), bf16[16,1,128,4,128]{4,2,0,1,3:T(8,128)(2,1)}, u32[]{:S(2)}, u32[]{:S(2)}) %all-to-all-start) | async-done | bytes 2097184 | tf_op jit(solution)/shard_map/all_to_all | solution.py:47
  53.5 6.7 %all-to-all-start.1 = ((bf16[8,64,16,128]{3,2,1,0:T(8,128)(2,1)}), bf16[8,64,16,128]{3,2,1,0:T(8,128)(2,1)S(1)}, u32[]{:S(2)}, u32[]{:S(2)}) async-start(bf16[8,64,16,128]{3,2,1,0:T(8,128)(2,1)} %reshape.182), calls=%async_computation.1 | async-start | bytes 4194304 | tf_op jit(solution)/shard_map/all_to_all | solution.py:71
  60.3 1.7 copy.48
  63.2 1.9 collective-permute-start
  66.7 2.8 %collective-permute-start.3 = (bf16[16,1,64,128]{3,2,1,0:T(8,128)(2,1)}, bf16[16,1,64,128]{3,2,1,0:T(8,128)(2,1)S(1)}, u32[]{:S(2)}, u32[]{:S(2)}) collective-permute-start(bf16[16,1,64,128]{3,2,1,0:T(8,128)(2,1)} %get-tuple-element.11), channel_id=1, source_target_pairs={{0,16},{4,20},{8,24},{12,28},{16,0},{20,4},{24,8},{28,12},{1,17},{... | collective-permute-start | bytes 786440 | tf_op jit(solution)/shard_map/ppermute | solution.py:67
  70.9 1.8 reshape.141
  73.7 10.4 %collective-permute-done = bf16[16,1,64,128]{3,2,1,0:T(8,128)(2,1)} collective-permute-done((bf16[16,1,64,128]{3,2,1,0:T(8,128)(2,1)}, bf16[16,1,64,128]{3,2,1,0:T(8,128)(2,1)}, u32[]{:S(2)}, u32[]{:S(2)}) %collective-permute-start) | collective-permute-done | bytes 262176 | tf_op jit(solution)/shard_map/ppermute | solution.py:67
  84.1 5.4 %collective-permute-start.5 = (bf16[16,1,64,128]{3,2,1,0:T(8,128)(2,1)S(1)}, bf16[16,1,64,128]{3,2,1,0:T(8,128)(2,1)S(1)}, u32[]{:S(2)}, u32[]{:S(2)}) collective-permute-start(bf16[16,1,64,128]{3,2,1,0:T(8,128)(2,1)S(1)} %get-tuple-element.9), channel_id=1, source_target_pairs={{0,24},{4,28},{8,16},{12,20},{16,8},{20,12},{24,0},{28,4},{1,25},{... | collective-permute-start | bytes 786440 | tf_op jit(solution)/shard_map/ppermute | solution.py:67
  89.5 1.8 copy_dynamic-update-slice_fusion.6
  91.3 10.7 %collective-permute-done.1 = bf16[16,1,64,128]{3,2,1,0:T(8,128)(2,1)S(1)} collective-permute-done((bf16[16,1,64,128]{3,2,1,0:T(8,128)(2,1)}, bf16[16,1,64,128]{3,2,1,0:T(8,128)(2,1)S(1)}, u32[]{:S(2)}, u32[]{:S(2)}) %collective-permute-start.1) | collective-permute-done | bytes 262176 | tf_op jit(solution)/shard_map/ppermute | solution.py:67
  102.0 3.8 %collective-permute-start.6 = (bf16[16,1,64,128]{3,2,1,0:T(8,128)(2,1)S(1)}, bf16[16,1,64,128]{3,2,1,0:T(8,128)(2,1)S(1)}, u32[]{:S(2)}, u32[]{:S(2)}) collective-permute-start(bf16[16,1,64,128]{3,2,1,0:T(8,128)(2,1)S(1)} %get-tuple-element.8), channel_id=1, source_target_pairs={{0,28},{4,24},{8,20},{12,16},{16,12},{20,8},{24,4},{28,0},{1,29},{... | collective-permute-start | bytes 786440 | tf_op jit(solution)/shard_map/ppermute | solution.py:67
  108.5 29.5 %collective-permute-done.3 = bf16[16,1,64,128]{3,2,1,0:T(8,128)(2,1)S(1)} collective-permute-done((bf16[16,1,64,128]{3,2,1,0:T(8,128)(2,1)}, bf16[16,1,64,128]{3,2,1,0:T(8,128)(2,1)S(1)}, u32[]{:S(2)}, u32[]{:S(2)}) %collective-permute-start.3) | collective-permute-done | bytes 262176 | tf_op jit(solution)/shard_map/ppermute | solution.py:67
  138.9 5.0 %collective-permute-done.4 = bf16[16,1,64,128]{3,2,1,0:T(8,128)(2,1)S(1)} collective-permute-done((bf16[16,1,64,128]{3,2,1,0:T(8,128)(2,1)}, bf16[16,1,64,128]{3,2,1,0:T(8,128)(2,1)S(1)}, u32[]{:S(2)}, u32[]{:S(2)}) %collective-permute-start.4) | collective-permute-done | bytes 262176 | tf_op jit(solution)/shard_map/ppermute | solution.py:67
  147.3 2.9 %convolution_bitcast_fusion = f32[128,128]{1,0:T(8,128)} fusion(bf16[128,64,128]{2,0,1:T(8,128)(2,1)} %copy_dynamic-update-slice_fusion, bf16[64,128,128]{2,1,0:T(8,128)(2,1)S(1)} %bitcast.81), kind=kOutput, calls=%fused_computation.10 | convolution fusion | flops 268435456 | bytes 4259840 | tf_op jit(solution)/shard_map/dot_general | solution.py:79
  151.5 65.7 %reduce-scatter.2.cloned.1.call-done = f32[16,128]{1,0:T(8,128)} async-done(((f32[128,128]{1,0:T(8,128)}), f32[16,128]{1,0:T(8,128)}) %reduce-scatter.2.cloned.1.call-update) | async-done | bytes 8208 | tf_op jit(solution)/shard_map/reduce_scatter | solution.py:82
  217.2 5.9 %all-reduce = f32[16,128]{1,0:T(8,128)S(1)} all-reduce(f32[16,128]{1,0:T(8,128)} %reduce-scatter.2.cloned.1.call-done), channel_id=3, replica_groups=mesh['grp'=8,'band'=4] {'band'}, use_global_device_ids=true, to_apply=%region_1.3.clone | all-reduce | flops 2048 | bytes 16384
  (49 shorter events, 22.8 us)
Async XLA Ops:
  6.5 6.3 %copy-start = (bf16[1,4,64,1024]{3,2,1,0:T(8,128)(2,1)S(1)}, bf16[1,4,64,1024]{3,2,1,0:T(8,128)(2,1)}, u32[]{:S(2)}) copy-start(bf16[1,4,64,1024]{3,2,1,0:T(8,128)(2,1)} %param.7) | copy-start | bytes 1572868
  6.5 4.6 %copy-start.1 = (bf16[512,512]{1,0:T(8,128)(2,1)S(1)}, bf16[512,512]{1,0:T(8,128)(2,1)}, u32[]{:S(2)}) copy-start(bf16[512,512]{1,0:T(8,128)(2,1)} %param.11) | copy-start | bytes 1572868
  22.7 30.8 %all-to-all-start = ((bf16[16,1,128,4,128]{4,2,0,1,3:T(8,128)(2,1)}), bf16[16,1,128,4,128]{4,2,0,1,3:T(8,128)(2,1)}, u32[]{:S(2)}, u32[]{:S(2)}) async-start(bf16[16,1,128,4,128]{4,2,0,1,3:T(8,128)(2,1)} %copy.47), calls=%async_computation | async-start | bytes 4194304 | tf_op jit(solution)/shard_map/all_to_all | solution.py:47
  53.5 93.1 %all-to-all-start.1 = ((bf16[8,64,16,128]{3,2,1,0:T(8,128)(2,1)}), bf16[8,64,16,128]{3,2,1,0:T(8,128)(2,1)S(1)}, u32[]{:S(2)}, u32[]{:S(2)}) async-start(bf16[8,64,16,128]{3,2,1,0:T(8,128)(2,1)} %reshape.182), calls=%async_computation.1 | async-start | bytes 4194304 | tf_op jit(solution)/shard_map/all_to_all | solution.py:71
  60.2 157.0 %reduce-scatter.2.cloned.1.call-start = ((), (), s32[]{:S(2)}) async-start(), calls=%async_computation.3 | async-start | bytes 73728 | tf_op jit(solution)/shard_map/reduce_scatter | solution.py:82
  63.2 20.9 %collective-permute-start = (bf16[16,1,64,128]{3,2,1,0:T(8,128)(2,1)}, bf16[16,1,64,128]{3,2,1,0:T(8,128)(2,1)}, u32[]{:S(2)}, u32[]{:S(2)}) collective-permute-start(bf16[16,1,64,128]{3,2,1,0:T(8,128)(2,1)} %get-tuple-element.14), channel_id=1, source_target_pairs={{0,4},{4,0},{8,12},{12,8},{16,20},{20,16},{24,28},{28,24},{1,5},{5... | collective-permute-start | bytes 786440 | tf_op jit(solution)/shard_map/ppermute | solution.py:67
  65.1 36.9 %collective-permute-start.1 = (bf16[16,1,64,128]{3,2,1,0:T(8,128)(2,1)}, bf16[16,1,64,128]{3,2,1,0:T(8,128)(2,1)S(1)}, u32[]{:S(2)}, u32[]{:S(2)}) collective-permute-start(bf16[16,1,64,128]{3,2,1,0:T(8,128)(2,1)} %get-tuple-element.13), channel_id=1, source_target_pairs={{0,8},{4,12},{8,0},{12,4},{16,24},{20,28},{24,16},{28,20},{1,9},{5... | collective-permute-start | bytes 786440 | tf_op jit(solution)/shard_map/ppermute | solution.py:67
  66.6 41.1 %collective-permute-start.2 = (bf16[16,1,64,128]{3,2,1,0:T(8,128)(2,1)}, bf16[16,1,64,128]{3,2,1,0:T(8,128)(2,1)S(1)}, u32[]{:S(2)}, u32[]{:S(2)}) collective-permute-start(bf16[16,1,64,128]{3,2,1,0:T(8,128)(2,1)} %get-tuple-element.12), channel_id=1, source_target_pairs={{0,12},{4,8},{8,4},{12,0},{16,28},{20,24},{24,20},{28,16},{1,13},{... | collective-permute-start | bytes 786440 | tf_op jit(solution)/shard_map/ppermute | solution.py:67
  66.7 71.3 %collective-permute-start.3 = (bf16[16,1,64,128]{3,2,1,0:T(8,128)(2,1)}, bf16[16,1,64,128]{3,2,1,0:T(8,128)(2,1)S(1)}, u32[]{:S(2)}, u32[]{:S(2)}) collective-permute-start(bf16[16,1,64,128]{3,2,1,0:T(8,128)(2,1)} %get-tuple-element.11), channel_id=1, source_target_pairs={{0,16},{4,20},{8,24},{12,28},{16,0},{20,4},{24,8},{28,12},{1,17},{... | collective-permute-start | bytes 786440 | tf_op jit(solution)/shard_map/ppermute | solution.py:67
  69.5 74.5 %collective-permute-start.4 = (bf16[16,1,64,128]{3,2,1,0:T(8,128)(2,1)}, bf16[16,1,64,128]{3,2,1,0:T(8,128)(2,1)S(1)}, u32[]{:S(2)}, u32[]{:S(2)}) collective-permute-start(bf16[16,1,64,128]{3,2,1,0:T(8,128)(2,1)} %get-tuple-element.10), channel_id=1, source_target_pairs={{0,20},{4,16},{8,28},{12,24},{16,4},{20,0},{24,12},{28,8},{1,21},{... | collective-permute-start | bytes 786440 | tf_op jit(solution)/shard_map/ppermute | solution.py:67
  84.1 60.8 %collective-permute-start.5 = (bf16[16,1,64,128]{3,2,1,0:T(8,128)(2,1)S(1)}, bf16[16,1,64,128]{3,2,1,0:T(8,128)(2,1)S(1)}, u32[]{:S(2)}, u32[]{:S(2)}) collective-permute-start(bf16[16,1,64,128]{3,2,1,0:T(8,128)(2,1)S(1)} %get-tuple-element.9), channel_id=1, source_target_pairs={{0,24},{4,28},{8,16},{12,20},{16,8},{20,12},{24,0},{28,4},{1,25},{... | collective-permute-start | bytes 786440 | tf_op jit(solution)/shard_map/ppermute | solution.py:67
  102.0 43.8 %collective-permute-start.6 = (bf16[16,1,64,128]{3,2,1,0:T(8,128)(2,1)S(1)}, bf16[16,1,64,128]{3,2,1,0:T(8,128)(2,1)S(1)}, u32[]{:S(2)}, u32[]{:S(2)}) collective-permute-start(bf16[16,1,64,128]{3,2,1,0:T(8,128)(2,1)S(1)} %get-tuple-element.8), channel_id=1, source_target_pairs={{0,28},{4,24},{8,20},{12,16},{16,12},{20,8},{24,4},{28,0},{1,29},{... | collective-permute-start | bytes 786440 | tf_op jit(solution)/shard_map/ppermute | solution.py:67
  147.3 3.0 %copy-start.2 = (u32[32]{0:T(128)S(1)}, u32[32]{0:T(128)}, u32[]{:S(2)}) copy-start(u32[32]{0:T(128)} %constant.79) | copy-start | bytes 388
Sparse Core Ops, SparseCore 0:
  150.4 66.7 reduce-scatter.1
